TPU v7x, 128 devices: a whole 4x4x4 slice. The times are simulated.
128 devices in a mesh: seq: 32 (over y, x, z_lo), chan: 4 (over z_hi, core).
Axes of the slice: x: 4, y: 4, z: 4 (z_hi: 2, z_lo: 2; z = z_hi * 2 + z_lo), core: 2. Of those that a mesh axis runs over, the one named last changes fastest.
Arguments:
- tokens: bfloat16 [24576, 4096], P('seq', 'chan'), may hold values from -4 to 4
- w_in: bfloat16 [8, 4096, 1296], P('chan', 'seq'), may hold values from -1 to 1
- conv_w: float32 [8, 4, 1280], P('chan'), may hold values from -3 to 3
- conv_b: float32 [8, 1280], P('chan'), may hold values from -3 to 3
- dt_bias: float32 [8, 16], P('chan'), may hold values from -8 to 2
- a_log: float32 [8, 16], P('chan'), may hold values from -4.6 to -3.7
- d_skip: float32 [8, 16], P('chan'), may hold values from 0.3 to 3
- norm_gain: float32 [8, 1024], P('chan'), may hold values from 0.5 to 1.5
Outputs:
- mixer_out: bfloat16 [24576, 8192], P('seq', 'chan')
All inputs are finite; a program needn't handle non-finite values.
Results may differ from a plain program's by a relative error of at most 0.0076.
Values may be sent and summed in bfloat16 or wider, within the bound.
No kernel may reach another device: no remote copies, remote signals or barrier semaphores. Data moves between devices by JAX's collectives and lax.ppermute only.
A program may use at most 128 MiB of HBM per device.

v0:
```python
import jax
import jax.numpy as jnp
from jax import lax
from jax.sharding import PartitionSpec as P

P_SIZE = 64
N = 128
KCONV = 4
Q = 128
HG = 16
GW = 1024
CW = 1280
epsilon = 1e-05


def shifted(block, axis, distance):
    devices = range(lax.axis_size(axis))
    route = [(i - distance, i) for i in devices if i - distance in devices]
    return lax.ppermute(block, axis, route)


def entering(keep, end, axis):
    place = lax.axis_index(axis)
    size = lax.axis_size(axis)
    keep = jnp.where(place == 0, 1.0, shifted(keep, axis, 1))
    end = shifted(end, axis, 1)
    distance = 1
    while distance < size:
        earlier_end = shifted(end, axis, distance)
        reach = place >= distance
        end = jnp.where(reach, keep[..., None, None] * earlier_end + end, end)
        if distance * 2 < size:
            earlier_keep = shifted(keep, axis, distance)
            keep = jnp.where(reach, keep * earlier_keep, keep)
        distance *= 2
    return end


def mix_groups(gathered, w_in, conv_w, conv_b, dt_bias, a_log, d_skip, norm_gain):
    groups = w_in.shape[0]
    row_count = gathered.shape[0]
    rows_first = jnp.transpose(w_in, (1, 0, 2))
    full_w = lax.all_gather(rows_first, "seq", axis=0, tiled=True)
    projected = jnp.einsum("td,dgc->tgc", gathered, full_w, preferred_element_type=jnp.float32)
    conv_in = projected[:, :, :CW].astype(jnp.bfloat16)
    raw_dt = projected[:, :, CW:]
    rim_rows = shifted(conv_in[row_count - (KCONV - 1) :], "seq", 1)
    padded = jnp.concatenate([rim_rows, conv_in], axis=0)
    pre_act = jnp.broadcast_to(conv_b[None], (row_count, groups, CW))
    for offset in range(KCONV):
        pre_act = pre_act + conv_w[None, :, offset] * padded[offset : offset + row_count]
    inputs = jax.nn.silu(pre_act).astype(jnp.bfloat16)
    block_count = row_count // Q
    blocked = inputs.reshape(block_count, Q, groups, CW)
    x_all = blocked[..., :GW].reshape(block_count, Q, groups, HG, P_SIZE)
    b_all = blocked[..., GW : GW + N]
    c_all = blocked[..., GW + N :]
    step_dt = jax.nn.softplus(raw_dt + dt_bias[None]).reshape(block_count, Q, groups, HG)
    decay_rate = -jnp.exp(a_log)
    cumulative = jnp.cumsum(decay_rate[None, None] * step_dt, axis=1)
    causal = lax.broadcasted_iota(jnp.int32, (Q, Q), 0) >= lax.broadcasted_iota(
        jnp.int32, (Q, Q), 1
    )
    last_cum = cumulative[:, -1]
    keep_all = jnp.exp(last_cum)
    tail_factor = jnp.exp(last_cum[:, None] - cumulative) * step_dt
    scaled = (x_all * tail_factor[..., None]).astype(jnp.bfloat16)
    fresh_all = jnp.einsum("qjghp,qjgn->qghpn", scaled, b_all, preferred_element_type=jnp.float32)
    local_states = []
    state_now = jnp.zeros(fresh_all.shape[1:], jnp.float32)
    keep_now = jnp.ones(keep_all.shape[1:], jnp.float32)
    keep_before = []
    for q in range(block_count):
        local_states.append(state_now)
        keep_before.append(keep_now)
        state_now = keep_all[q][..., None, None] * state_now + fresh_all[q]
        keep_now = keep_now * keep_all[q]
    incoming = entering(keep_now, state_now, "seq")
    states = jnp.stack(local_states) + jnp.stack(keep_before)[..., None, None] * incoming[None]
    scores = jnp.einsum("qign,qjgn->qgij", c_all, b_all, preferred_element_type=jnp.float32)
    cum_cols = jnp.transpose(cumulative, (0, 2, 3, 1))
    dt_cols = jnp.transpose(step_dt, (0, 2, 3, 1))
    spread = cum_cols[..., :, None] - cum_cols[..., None, :]
    damping = jnp.where(causal, jnp.exp(jnp.minimum(spread, 0.0)), 0.0)
    weights = (scores[:, :, None] * damping * dt_cols[..., None, :]).astype(jnp.bfloat16)
    partial_y = jnp.einsum("qghij,qjghp->qighp", weights, x_all, preferred_element_type=jnp.float32)
    partial_y = partial_y + d_skip[None, None, :, :, None] * x_all
    across = jnp.einsum(
        "qign,qghpn->qighp", c_all, states.astype(jnp.bfloat16), preferred_element_type=jnp.float32
    )
    activity = partial_y + jnp.exp(cumulative)[..., None] * across
    flat_act = activity.reshape(row_count, groups, GW)
    inv_rms = lax.rsqrt(jnp.mean(flat_act * flat_act, axis=-1, keepdims=True) + epsilon)
    normed = (flat_act * inv_rms * norm_gain[None]).astype(jnp.bfloat16)
    return normed.reshape(row_count, groups * GW)


def per_device(tokens, w_in, conv_w, conv_b, dt_bias, a_log, d_skip, norm_gain):
    gathered = lax.all_gather(tokens, "chan", axis=1, tiled=True)
    return mix_groups(gathered, w_in, conv_w, conv_b, dt_bias, a_log, d_skip, norm_gain)


def solution(mesh):
    return jax.shard_map(
        per_device,
        mesh=mesh,
        in_specs=(
            P("seq", "chan"),
            P("chan", "seq", None),
            P("chan", None, None),
            P("chan", None),
            P("chan", None),
            P("chan", None),
            P("chan", None),
            P("chan", None),
        ),
        out_specs=P("seq", "chan"),
        check_vma=False,
    )
```

profile of v0, /device:TPU:80, one launch (start us, length us, event | category | flops | bytes accessed | tf_op | source)
XLA Modules:
  0.0 843.2 jit_solution(2859440067428863867)
XLA Ops:
  9.7 48.6 %all-gather.3.cloned.1.call-done = bf16[768,4096]{1,0:T(8,128)(2,1)} async-done(((bf16[768,1024]{1,0:T(8,128)(2,1)}), bf16[768,4096]{1,0:T(8,128)(2,1)}) %all-gather.3.cloned.1.call-update) | async-done | bytes 6291472 | tf_op jit(solution)/shard_map/all_gather | solution.py:99
  58.3 513.7 %all-gather.5.cloned.1.call-done = bf16[4096,2,1296]{0,2,1:T(8,128)(2,1)} async-done(((bf16[128,2,1296]{0,2,1:T(8,128)(2,1)}), bf16[4096,2,1296]{0,2,1:T(8,128)(2,1)}) %all-gather.5.cloned.1.call-update) | async-done | bytes 21233680 | tf_op jit(solution)/shard_map/all_gather | solution.py:43
  572.1 22.7 %fusion.45 = (bf16[768,2,1296]{0,2,1:T(8,128)(2,1)}, f32[768,2,1296]{0,2,1:T(8,128)S(1)}) fusion(bf16[4096,2,1296]{0,2,1:T(8,128)(2,1)} %all-gather.5.cloned.1.call-done, bf16[768,4096]{1,0:T(8,128)(2,1)} %all-gather.3.cloned.1.call-done), kind=kOutput, calls=%fused_computation.110 | convolution fusion | flops 16309444608 | bytes 39469056 | tf_op jit(solution)/shard_map/td,dgc->tgc/dot_general | solution.py:44
  598.3 7.9 collective-permute-start
  608.6 4.3 slice.113
  614.2 14.2 %multiply_convert_fusion.1 = bf16[768,2,1280]{0,2,1:T(8,128)(2,1)} fusion(bf16[768,2,1280]{0,2,1:T(8,128)(2,1)} %slice.113, bf16[3,2,1280]{0,2,1:T(8,128)(2,1)S(1)} %copy.46, f32[2,1280]{1,0:T(2,128)S(1)} %get-tuple-element.31, f32[2,1280]{1,0:T(2,128)S(1)} %get-tuple-element.32, f32[2,1280]{1,0:T(2,128)S(1)} %get-tuple-element.33, ...), kind=kLoop, calls=%fused_computation.3 | loop fusion | flops 51118080 | bytes 7930880 | tf_op jit(solution)/shard_map/convert_element_type | solution.py:52
  628.4 6.3 copy.47
  634.7 3.9 slice.118
  638.6 2.0 fusion.43
  640.5 3.5 copy.48
  644.1 2.0 fusion.17
  646.1 2.7 copy-done
  649.3 2.5 collective-permute-start.6
  651.8 26.3 %collective-permute-done.6 = f32[2,16,64,128]{3,2,1,0:T(8,128)} collective-permute-done((f32[2,16,64,128]{3,2,1,0:T(8,128)S(1)}, f32[2,16,64,128]{3,2,1,0:T(8,128)}, u32[]{:S(2)}, u32[]{:S(2)}) %collective-permute-start.6) | collective-permute-done | bytes 1048608 | tf_op jit(solution)/shard_map/ppermute | solution.py:19
  678.0 3.9 collective-permute-start.7
  682.0 5.4 collective-permute-start.1
  687.4 21.5 %collective-permute-done.1 = f32[2,16]{1,0:T(2,128)S(1)} collective-permute-done((f32[2,16]{1,0:T(2,128)}, f32[2,16]{1,0:T(2,128)S(1)}, u32[]{:S(2)}, u32[]{:S(2)}) %collective-permute-start.1) | collective-permute-done | bytes 160 | tf_op jit(solution)/shard_map/ppermute | solution.py:19
  710.9 3.9 collective-permute-start.8
  718.6 22.0 %collective-permute-done.2 = f32[2,16]{1,0:T(2,128)S(1)} collective-permute-done((f32[2,16]{1,0:T(2,128)}, f32[2,16]{1,0:T(2,128)S(1)}, u32[]{:S(2)}, u32[]{:S(2)}) %collective-permute-start.2) | collective-permute-done | bytes 160 | tf_op jit(solution)/shard_map/ppermute | solution.py:19
  743.5 1.9 collective-permute-start.9
  746.1 2.1 collective-permute-start.3
  750.1 7.7 collective-permute-done.3
  758.5 3.1 collective-permute-start.4
  763.2 3.2 collective-permute-done.4
  773.3 2.6 fusion.28
  779.2 2.7 constant_dynamic-update-slice_fusion.1
  785.7 17.3 %collective-permute-done.10 = f32[2,16,64,128]{3,2,1,0:T(8,128)S(1)} collective-permute-done((f32[2,16,64,128]{3,2,1,0:T(8,128)S(1)}, f32[2,16,64,128]{3,2,1,0:T(8,128)S(1)}, u32[]{:S(2)}, u32[]{:S(2)}) %collective-permute-start.10) | collective-permute-done | bytes 1048608 | tf_op jit(solution)/shard_map/ppermute | solution.py:19
  805.7 8.7 %fusion = f32[6,2,16,64,128]{4,3,2,1,0:T(8,128)} fusion(bf16[6,128,2,16,64]{1,4,3,2,0:T(8,128)(2,1)S(1)} %bitcast.132, f32[6,2,16,128]{3,2,1,0:T(8,128)S(1)} %copy-done.9, f32[6,2,16,128]{3,2,1,0:T(8,128)S(1)} %copy-done.8, f32[6,2,128,128]{3,2,1,0:T(8,128)S(1)} %fusion.32, pred[128,128]{1,0:T(8,128)(4,1)S(1)} %copy-done.10), kind=kOutput, calls=%fused_computation.4 | convolution fusion | flops 421527552 | bytes 10436608 | tf_op jit(solution)/shard_map/qghij,qjghp->qighp/dot_general | solution.py:86
  814.4 7.7 collective-permute-done.11
  822.4 4.4 multiply_reduce_fusion
  826.7 5.6 copy.58
  833.4 2.9 copy.59
  (117 shorter events, 42.2 us)
Async XLA Ops:
  6.5 51.8 %all-gather.3.cloned.1.call-start = ((), (), s32[]{:S(2)}) async-start(), calls=%async_computation | async-start | bytes 7864320 | tf_op jit(solution)/shard_map/all_gather | solution.py:99
  7.3 564.8 %all-gather.5.cloned.1.call-start = ((), (), s32[]{:S(2)}) async-start(), calls=%async_computation.1 | async-start | bytes 21897216 | tf_op jit(solution)/shard_map/all_gather | solution.py:43
  9.7 585.0 %copy-start.22 = (f32[2,16]{1,0:T(2,128)S(1)}, f32[2,16]{1,0:T(2,128)}, u32[]{:S(2)}) copy-start(f32[2,16]{1,0:T(2,128)} %param.12) | copy-start | bytes 388
  595.6 17.2 %copy-start.3 = (f32[6,128,2,16]{3,2,1,0:T(2,128)}, f32[6,128,2,16]{3,2,1,0:T(2,128)S(1)}, u32[]{:S(2)}) copy-start(f32[6,128,2,16]{3,2,1,0:T(2,128)S(1)} %fusion.46) | copy-start | bytes 294916
  598.3 15.9 %copy-start.11 = (f32[2,1280]{1,0:T(2,128)S(1)}, f32[2,1280]{1,0:T(2,128)}, u32[]{:S(2)}) copy-start(f32[2,1280]{1,0:T(2,128)} %param.11) | copy-start | bytes 30724
  598.3 15.5 %collective-permute-start = (bf16[3,2,1280]{2,1,0:T(2,128)(2,1)S(1)}, bf16[3,2,1280]{2,1,0:T(2,128)(2,1)S(1)}, u32[]{:S(2)}, u32[]{:S(2)}) collective-permute-start(bf16[3,2,1280]{2,1,0:T(2,128)(2,1)S(1)} %copy.45), channel_id=1, source_target_pairs={{0,4},{4,8},{8,12},{12,16},{16,20},{20,24},{24,28},{28,32},{32,36}... | collective-permute-start | bytes 46088 | tf_op jit(solution)/shard_map/ppermute | solution.py:19
  608.6 19.8 %copy-start.18 = (f32[6,2,16]{2,1,0:T(2,128)}, f32[6,2,16]{2,1,0:T(2,128)S(1)}, u32[]{:S(2)}) copy-start(f32[6,2,16]{2,1,0:T(2,128)S(1)} %get-tuple-element.19) | copy-start | bytes 2308
  608.6 37.5 %copy-start.13 = (f32[2,16]{1,0:T(2,128)}, f32[2,16]{1,0:T(2,128)S(1)}, u32[]{:S(2)}) copy-start(f32[2,16]{1,0:T(2,128)S(1)} %get-tuple-element.21) | copy-start | bytes 388
  608.6 37.5 %copy-start.15 = (f32[2,16]{1,0:T(2,128)}, f32[2,16]{1,0:T(2,128)S(1)}, u32[]{:S(2)}) copy-start(f32[2,16]{1,0:T(2,128)S(1)} %get-tuple-element.22) | copy-start | bytes 388
  649.3 28.8 %collective-permute-start.6 = (f32[2,16,64,128]{3,2,1,0:T(8,128)S(1)}, f32[2,16,64,128]{3,2,1,0:T(8,128)}, u32[]{:S(2)}, u32[]{:S(2)}) collective-permute-start(f32[2,16,64,128]{3,2,1,0:T(8,128)S(1)} %fusion.22), channel_id=1, source_target_pairs={{0,4},{4,8},{8,12},{12,16},{16,20},{20,24},{24,28},{28,32},{32,36}... | collective-permute-start | bytes 3145736 | tf_op jit(solution)/shard_map/ppermute | solution.py:19
  678.0 31.5 %collective-permute-start.7 = (f32[2,16,64,128]{3,2,1,0:T(8,128)}, f32[2,16,64,128]{3,2,1,0:T(8,128)S(1)}, u32[]{:S(2)}, u32[]{:S(2)}) collective-permute-start(f32[2,16,64,128]{3,2,1,0:T(8,128)} %collective-permute-done.6), channel_id=1, source_target_pairs={{0,4},{4,8},{8,12},{12,16},{16,20},{20,24},{24,28},{28,32},{32,36}... | collective-permute-start | bytes 3145736 | tf_op jit(solution)/shard_map/ppermute | solution.py:19
  682.0 26.9 %collective-permute-start.1 = (f32[2,16]{1,0:T(2,128)}, f32[2,16]{1,0:T(2,128)S(1)}, u32[]{:S(2)}, u32[]{:S(2)}) collective-permute-start(f32[2,16]{1,0:T(2,128)} %get-tuple-element.25), channel_id=1, source_target_pairs={{0,4},{4,8},{8,12},{12,16},{16,20},{20,24},{24,28},{28,32},{32,36}... | collective-permute-start | bytes 392 | tf_op jit(solution)/shard_map/ppermute | solution.py:19
  710.9 30.9 %copy-start.4 = (f32[2,16,64,128]{3,2,1,0:T(8,128)}, f32[2,16,64,128]{3,2,1,0:T(8,128)S(1)}, u32[]{:S(2)}) copy-start(f32[2,16,64,128]{3,2,1,0:T(8,128)S(1)} %add_select_fusion.4) | copy-start | bytes 3145732
  710.9 30.9 %collective-permute-start.8 = (f32[2,16,64,128]{3,2,1,0:T(8,128)S(1)}, f32[2,16,64,128]{3,2,1,0:T(8,128)}, u32[]{:S(2)}, u32[]{:S(2)}) collective-permute-start(f32[2,16,64,128]{3,2,1,0:T(8,128)S(1)} %add_select_fusion.4), channel_id=1, source_target_pairs={{0,8},{4,12},{8,16},{12,20},{16,24},{20,28},{24,32},{28,36},{32,40... | collective-permute-start | bytes 3145736 | tf_op jit(solution)/shard_map/ppermute | solution.py:19
  714.8 67.1 %slice-start = ((s8[6291456]{0:T(1024)(128)(4,1)}), s8[2097152]{0:T(1024)(128)(4,1)S(1)}, s32[]{:S(2)}) async-start(s8[6291456]{0:T(1024)(128)(4,1)} %bitcast.128), calls=%async_computation.2 | async-start | bytes 4194304
  715.9 24.6 %collective-permute-start.2 = (f32[2,16]{1,0:T(2,128)}, f32[2,16]{1,0:T(2,128)S(1)}, u32[]{:S(2)}, u32[]{:S(2)}) collective-permute-start(f32[2,16]{1,0:T(2,128)} %broadcast_select_fusion), channel_id=1, source_target_pairs={{0,4},{4,8},{8,12},{12,16},{16,20},{20,24},{24,28},{28,32},{32,36}... | collective-permute-start | bytes 392 | tf_op jit(solution)/shard_map/ppermute | solution.py:19
  743.5 32.3 %collective-permute-start.9 = (f32[2,16,64,128]{3,2,1,0:T(8,128)S(1)}, f32[2,16,64,128]{3,2,1,0:T(8,128)}, u32[]{:S(2)}, u32[]{:S(2)}) collective-permute-start(f32[2,16,64,128]{3,2,1,0:T(8,128)S(1)} %add_select_fusion.3), channel_id=1, source_target_pairs={{0,16},{4,20},{8,24},{12,28},{16,32},{20,36},{24,40},{28,44},{32,4... | collective-permute-start | bytes 3145736 | tf_op jit(solution)/shard_map/ppermute | solution.py:19
  746.1 11.7 %collective-permute-start.3 = (f32[2,16]{1,0:T(2,128)}, f32[2,16]{1,0:T(2,128)}, u32[]{:S(2)}, u32[]{:S(2)}) collective-permute-start(f32[2,16]{1,0:T(2,128)} %multiply_select_fusion.3), channel_id=1, source_target_pairs={{0,8},{4,12},{8,16},{12,20},{16,24},{20,28},{24,32},{28,36},{32,40... | collective-permute-start | bytes 392 | tf_op jit(solution)/shard_map/ppermute | solution.py:19
  758.5 7.9 collective-permute-start.4
  766.9 5.7 collective-permute-start.5
  777.3 25.8 %collective-permute-start.10 = (f32[2,16,64,128]{3,2,1,0:T(8,128)S(1)}, f32[2,16,64,128]{3,2,1,0:T(8,128)S(1)}, u32[]{:S(2)}, u32[]{:S(2)}) collective-permute-start(f32[2,16,64,128]{3,2,1,0:T(8,128)S(1)} %add_select_fusion.2), channel_id=1, source_target_pairs={{0,32},{4,36},{8,40},{12,44},{16,48},{20,52},{24,56},{28,60},{32,6... | collective-permute-start | bytes 3145736 | tf_op jit(solution)/shard_map/ppermute | solution.py:19
  783.1 22.1 %copy-start.5 = (bf16[6,128,2,128]{3,1,0,2:T(8,128)(2,1)S(1)}, bf16[6,128,2,128]{3,1,0,2:T(8,128)(2,1)}, u32[]{:S(2)}) copy-start(bf16[6,128,2,128]{3,1,0,2:T(8,128)(2,1)} %get-tuple-element.11) | copy-start | bytes 1179652
  783.2 22.5 %copy-start.2 = (bf16[6,128,2,1024]{1,3,2,0:T(8,128)(2,1)S(1)}, bf16[6,128,2,1024]{1,3,2,0:T(8,128)(2,1)}, u32[]{:S(2)}) copy-start(bf16[6,128,2,1024]{1,3,2,0:T(8,128)(2,1)} %copy-done.1) | copy-start | bytes 9437188
  783.2 22.5 %copy-start.8 = (f32[6,2,16,128]{3,2,1,0:T(8,128)S(1)}, f32[6,2,16,128]{3,2,1,0:T(8,128)}, u32[]{:S(2)}) copy-start(f32[6,2,16,128]{3,2,1,0:T(8,128)} %copy.52) | copy-start | bytes 294916
  783.2 22.5 %copy-start.9 = (f32[6,2,16,128]{3,2,1,0:T(8,128)S(1)}, f32[6,2,16,128]{3,2,1,0:T(8,128)}, u32[]{:S(2)}) copy-start(f32[6,2,16,128]{3,2,1,0:T(8,128)} %copy.54) | copy-start | bytes 294916
  783.2 22.5 %copy-start.10 = (pred[128,128]{1,0:T(8,128)(4,1)S(1)}, pred[128,128]{1,0:T(8,128)(4,1)}, u32[]{:S(2)}) copy-start(pred[128,128]{1,0:T(8,128)(4,1)} %iota_compare_fusion) | copy-start | bytes 49156
  803.9 18.2 %collective-permute-start.11 = (f32[2,16,64,128]{3,2,1,0:T(8,128)S(1)}, f32[2,16,64,128]{3,2,1,0:T(8,128)S(1)}, u32[]{:S(2)}, u32[]{:S(2)}) collective-permute-start(f32[2,16,64,128]{3,2,1,0:T(8,128)S(1)} %add_select_fusion.1), channel_id=1, source_target_pairs={{0,64},{4,68},{8,72},{12,76},{16,80},{20,84},{24,88},{28,92},{32,9... | collective-permute-start | bytes 3145736 | tf_op jit(solution)/shard_map/ppermute | solution.py:19
  805.2 17.1 %slice-start.2 = ((s8[6291456]{0:T(1024)(128)(4,1)}), s8[4194304]{0:T(1024)(128)(4,1)S(1)}, s32[]{:S(2)}) async-start(s8[6291456]{0:T(1024)(128)(4,1)} %bitcast.136), calls=%async_computation.4 | async-start | bytes 8388608
  805.7 16.7 %slice-start.3 = ((s8[6291456]{0:T(1024)(128)(4,1)}), s8[2097152]{0:T(1024)(128)(4,1)S(1)}, s32[]{:S(2)}) async-start(s8[6291456]{0:T(1024)(128)(4,1)} %bitcast.136), calls=%async_computation.5 | async-start | bytes 4194304
  805.7 16.7 %copy-start.7 = (f32[6,128,2,16]{1,3,2,0:T(8,128)S(1)}, f32[6,128,2,16]{1,3,2,0:T(8,128)}, u32[]{:S(2)}) copy-start(f32[6,128,2,16]{1,3,2,0:T(8,128)} %copy.55) | copy-start | bytes 294916
  805.7 16.7 %copy-start.19 = (f32[6,2,16]{2,1,0:T(2,128)S(1)}, f32[6,2,16]{2,1,0:T(2,128)}, u32[]{:S(2)}) copy-start(f32[6,2,16]{2,1,0:T(2,128)} %copy-done.18) | copy-start | bytes 2308
  805.7 16.7 %copy-start.23 = (f32[2,16]{1,0:T(2,128)S(1)}, f32[2,16]{1,0:T(2,128)}, u32[]{:S(2)}) copy-start(f32[2,16]{1,0:T(2,128)} %param.14) | copy-start | bytes 388
  (10 other events, 61.6 us)
Sparse Core Ops, SparseCore 0:
  9.0 49.2 all-gather.2
  59.9 512.1 all-gather.4
where the time goes:
time: 844 us; the launch traced here: 843 us
  waiting for transfers between devices  671 us (80%)
  local copies, waits for them, and re-layouts  43 us (5%)
  other arithmetic  38.9 us (5%)
  matrix products  38.1 us (5%)
  starting transfers between devices  37.9 us (4%)
  between operations  14 us (2%)
    all_gather x1, waiting for transfers between devices, mix_groups(): full_w = lax.all_gather(rows_first, 'seq', axis=0, tiled=True)  514 us
    ppermute x12, waiting for transfers between devices, shifted(): return lax.ppermute(block, axis, route)  108 us
    all_gather x1, waiting for transfers between devices, per_device(): gathered = lax.all_gather(tokens, 'chan', axis=1, tiled=True)  48.6 us
    ppermute x12, starting transfers between devices, shifted(): return lax.ppermute(block, axis, route)  37.8 us
    dot_general x1, matrix products, mix_groups(): jnp.einsum('td,dgc->tgc', gathered, full_w, preferred_element_type=jnp.fl...  22.7 us
  transfers between devices with their start and end apart: 14, of which 10 were waited for; matrix products, arithmetic and copies ran while one was open for 5% of the time, Pallas kernels for 0%

commit v1 on v0

--- a/solution.py
+++ b/solution.py
@@ -96,7 +96,10 @@
 
 
 def per_device(tokens, w_in, conv_w, conv_b, dt_bias, a_log, d_skip, norm_gain):
-    gathered = lax.all_gather(tokens, "chan", axis=1, tiled=True)
+    devices_2 = lax.axis_size("chan")
+    blocks = jnp.stack([tokens for _ in range(devices_2)])
+    blocks = lax.all_to_all(blocks, "chan", split_axis=0, concat_axis=0)
+    gathered = jnp.concatenate(blocks, axis=1)
     return mix_groups(gathered, w_in, conv_w, conv_b, dt_bias, a_log, d_skip, norm_gain)
 
 

time: 844 us -> 807 us (0.956)
  waiting for transfers between devices: 671 us -> 609 us
  local copies, waits for them, and re-layouts: 43 us -> 68.4 us
    all_gather x1, waiting for transfers between devices: 514 us -> 295 us  [mix_groups(): full_w = lax.all_gather(rows_first, 'seq', axis=0, tiled=True)]
    all_to_all x0 -> x1, waiting for transfers between devices: none -> 199 us  [per_device(): blocks = lax.all_to_all(blocks, 'chan', split_axis=0, concat_axis=0)]
    all_gather x1 -> x0, waiting for transfers between devices: 48.6 us -> none  [per_device(): gathered = lax.all_gather(tokens, 'chan', axis=1, tiled=True)]
    reshape x0 -> x2, local copies, waits for them, and re-layouts: none -> 21.4 us  [per_device(): gathered = jnp.concatenate(blocks, axis=1)]
  transfers between devices with their start and end apart: 14 -> 14, of which waited for: 10 -> 11; matrix products, arithmetic and copies ran while one was open for 5% -> 8% of each run, Pallas kernels for 0% -> 0%
where the time goes in v1:
time: 807 us; the launch traced here: 804 us
  waiting for transfers between devices  609 us (75%)
  local copies, waits for them, and re-layouts  68.4 us (8%)
  other arithmetic  38.3 us (5%)
  matrix products  38.1 us (5%)
  starting transfers between devices  36.7 us (5%)
  between operations  14 us (2%)
    all_gather x1, waiting for transfers between devices, mix_groups(): full_w = lax.all_gather(rows_first, 'seq', axis=0, tiled=True)  295 us
    all_to_all x1, waiting for transfers between devices, per_device(): blocks = lax.all_to_all(blocks, 'chan', split_axis=0, concat_axis=0)  199 us
    ppermute x12, waiting for transfers between devices, shifted(): return lax.ppermute(block, axis, route)  114 us
    ppermute x12, starting transfers between devices, shifted(): return lax.ppermute(block, axis, route)  31.3 us
    dot_general x1, matrix products, mix_groups(): jnp.einsum('td,dgc->tgc', gathered, full_w, preferred_element_type=jnp.fl...  22.7 us
    reshape x2, local copies, waits for them, and re-layouts, per_device(): gathered = jnp.concatenate(blocks, axis=1)  21.4 us
  transfers between devices with their start and end apart: 14, of which 11 were waited for; matrix products, arithmetic and copies ran while one was open for 8% of the time, Pallas kernels for 0%

profile of v1, /device:TPU:80, one launch (start us, length us, event | category | flops | bytes accessed | tf_op | source)
XLA Modules:
  0.0 804.5 jit_solution(8798290046050220265)
XLA Ops:
  7.3 4.9 stack.6
  12.2 5.4 all-to-all-start
  17.7 199.2 %all-to-all-done = bf16[4,768,1024]{2,1,0:T(8,128)(2,1)} async-done(((bf16[4,768,1024]{2,1,0:T(8,128)(2,1)}), bf16[4,768,1024]{2,1,0:T(8,128)(2,1)}, u32[]{:S(2)}, u32[]{:S(2)}) %all-to-all-start) | async-done | bytes 6291488 | tf_op jit(solution)/shard_map/all_to_all | solution.py:101
  216.9 10.3 %copy.45 = bf16[768,4,1024]{2,1,0:T(4,128)(2,1)} copy(bf16[768,4,1024]{2,0,1:T(8,128)(2,1)} %bitcast) | data formatting | bytes 12582912 | tf_op jit(solution)/shard_map/reshape | solution.py:102
  227.2 11.1 %reshape.86 = bf16[768,4096,1]{1,0,2:T(8,128)(2,1)} reshape(bf16[768,4,1024]{2,1,0:T(4,128)(2,1)} %copy.45) | data formatting | bytes 12582912 | tf_op jit(solution)/shard_map/reshape | solution.py:102
  238.3 294.7 %all-gather.2.cloned.1.call-done = bf16[4096,2,1296]{0,2,1:T(8,128)(2,1)} async-done(((bf16[128,2,1296]{0,2,1:T(8,128)(2,1)}), bf16[4096,2,1296]{0,2,1:T(8,128)(2,1)}) %all-gather.2.cloned.1.call-update) | async-done | bytes 21233680 | tf_op jit(solution)/shard_map/all_gather | solution.py:43
  533.0 22.7 %fusion.43 = (bf16[768,2,1296]{0,2,1:T(8,128)(2,1)}, f32[768,2,1296]{0,2,1:T(8,128)S(1)}) fusion(bf16[768,4096,1]{1,0,2:T(8,128)(2,1)} %reshape.86, bf16[4096,2,1296]{0,2,1:T(8,128)(2,1)} %all-gather.2.cloned.1.call-done), kind=kOutput, calls=%fused_computation.108 | convolution fusion | flops 16309444608 | bytes 39469056 | tf_op jit(solution)/shard_map/td,dgc->tgc/dot_general | solution.py:44
  559.2 2.9 collective-permute-start
  564.5 4.3 slice.113
  570.1 14.3 %multiply_convert_fusion.1 = bf16[768,2,1280]{0,2,1:T(8,128)(2,1)} fusion(bf16[768,2,1280]{0,2,1:T(8,128)(2,1)} %slice.113, bf16[3,2,1280]{0,2,1:T(8,128)(2,1)S(1)} %copy.47, f32[2,1280]{1,0:T(2,128)S(1)} %get-tuple-element.31, f32[2,1280]{1,0:T(2,128)S(1)} %get-tuple-element.32, f32[2,1280]{1,0:T(2,128)S(1)} %get-tuple-element.33, ...), kind=kLoop, calls=%fused_computation.3 | loop fusion | flops 51118080 | bytes 7930880 | tf_op jit(solution)/shard_map/convert_element_type | solution.py:52
  584.4 6.4 copy.48
  590.8 3.9 slice.118
  594.7 1.9 fusion.41
  596.6 3.5 copy.49
  600.1 2.0 fusion.15
  602.2 2.7 copy-done
  607.2 28.3 %collective-permute-done.6 = f32[2,16,64,128]{3,2,1,0:T(8,128)} collective-permute-done((f32[2,16,64,128]{3,2,1,0:T(8,128)S(1)}, f32[2,16,64,128]{3,2,1,0:T(8,128)}, u32[]{:S(2)}, u32[]{:S(2)}) %collective-permute-start.6) | collective-permute-done | bytes 1048608 | tf_op jit(solution)/shard_map/ppermute | solution.py:19
  639.4 25.5 %collective-permute-done.1 = f32[2,16]{1,0:T(2,128)S(1)} collective-permute-done((f32[2,16]{1,0:T(2,128)}, f32[2,16]{1,0:T(2,128)S(1)}, u32[]{:S(2)}, u32[]{:S(2)}) %collective-permute-start.1) | collective-permute-done | bytes 160 | tf_op jit(solution)/shard_map/ppermute | solution.py:19
  672.6 18.6 %collective-permute-done.2 = f32[2,16]{1,0:T(2,128)S(1)} collective-permute-done((f32[2,16]{1,0:T(2,128)}, f32[2,16]{1,0:T(2,128)S(1)}, u32[]{:S(2)}, u32[]{:S(2)}) %collective-permute-start.2) | collective-permute-done | bytes 160 | tf_op jit(solution)/shard_map/ppermute | solution.py:19
  698.5 2.3 collective-permute-start.3
  702.7 15.3 %collective-permute-done.3 = f32[2,16]{1,0:T(2,128)} collective-permute-done((f32[2,16]{1,0:T(2,128)}, f32[2,16]{1,0:T(2,128)}, u32[]{:S(2)}, u32[]{:S(2)}) %collective-permute-start.3) | collective-permute-done | bytes 160 | tf_op jit(solution)/shard_map/ppermute | solution.py:19
  718.7 6.1 collective-permute-start.4
  727.1 3.5 collective-permute-start.5
  733.4 2.6 fusion.26
  737.4 3.5 collective-permute-start.10
  740.9 2.7 constant_dynamic-update-slice_fusion.1
  747.3 12.3 %collective-permute-done.10 = f32[2,16,64,128]{3,2,1,0:T(8,128)S(1)} collective-permute-done((f32[2,16,64,128]{3,2,1,0:T(8,128)S(1)}, f32[2,16,64,128]{3,2,1,0:T(8,128)S(1)}, u32[]{:S(2)}, u32[]{:S(2)}) %collective-permute-start.10) | collective-permute-done | bytes 1048608 | tf_op jit(solution)/shard_map/ppermute | solution.py:19
  762.6 8.7 %fusion = f32[6,2,16,64,128]{4,3,2,1,0:T(8,128)} fusion(bf16[6,128,2,16,64]{1,4,3,2,0:T(8,128)(2,1)S(1)} %bitcast.129, f32[6,2,16,128]{3,2,1,0:T(8,128)S(1)} %copy-done.9, f32[6,2,16,128]{3,2,1,0:T(8,128)S(1)} %copy-done.8, f32[6,2,128,128]{3,2,1,0:T(8,128)S(1)} %fusion.30, pred[128,128]{1,0:T(8,128)(4,1)S(1)} %copy-done.11), kind=kOutput, calls=%fused_computation.4 | convolution fusion | flops 421527552 | bytes 10436608 | tf_op jit(solution)/shard_map/qghij,qjghp->qighp/dot_general | solution.py:86
  771.3 12.2 %collective-permute-done.11 = f32[2,16,64,128]{3,2,1,0:T(8,128)S(1)} collective-permute-done((f32[2,16,64,128]{3,2,1,0:T(8,128)S(1)}, f32[2,16,64,128]{3,2,1,0:T(8,128)S(1)}, u32[]{:S(2)}, u32[]{:S(2)}) %collective-permute-start.11) | collective-permute-done | bytes 1048608 | tf_op jit(solution)/shard_map/ppermute | solution.py:19
  783.7 4.4 multiply_reduce_fusion
  788.0 5.6 copy.59
  794.8 2.9 copy.60
  (123 shorter events, 46.2 us)
Async XLA Ops:
  6.5 526.5 %all-gather.2.cloned.1.call-start = ((), (), s32[]{:S(2)}) async-start(), calls=%async_computation.1 | async-start | bytes 21897216 | tf_op jit(solution)/shard_map/all_gather | solution.py:43
  12.2 204.7 %all-to-all-start = ((bf16[4,768,1024]{2,1,0:T(8,128)(2,1)}), bf16[4,768,1024]{2,1,0:T(8,128)(2,1)}, u32[]{:S(2)}, u32[]{:S(2)}) async-start(bf16[4,768,1024]{2,1,0:T(8,128)(2,1)} %stack.6), calls=%async_computation | async-start | bytes 12582912 | tf_op jit(solution)/shard_map/all_to_all | solution.py:101
  238.3 317.3 %copy-start.23 = (f32[2,16]{1,0:T(2,128)S(1)}, f32[2,16]{1,0:T(2,128)}, u32[]{:S(2)}) copy-start(f32[2,16]{1,0:T(2,128)} %param.12) | copy-start | bytes 388
  556.6 12.2 %copy-start.3 = (f32[6,128,2,16]{3,2,1,0:T(2,128)}, f32[6,128,2,16]{3,2,1,0:T(2,128)S(1)}, u32[]{:S(2)}) copy-start(f32[6,128,2,16]{3,2,1,0:T(2,128)S(1)} %fusion.44) | copy-start | bytes 294916
  559.2 10.5 %collective-permute-start = (bf16[3,2,1280]{2,1,0:T(2,128)(2,1)S(1)}, bf16[3,2,1280]{2,1,0:T(2,128)(2,1)S(1)}, u32[]{:S(2)}, u32[]{:S(2)}) collective-permute-start(bf16[3,2,1280]{2,1,0:T(2,128)(2,1)S(1)} %copy.46), channel_id=1, source_target_pairs={{0,4},{4,8},{8,12},{12,16},{16,20},{20,24},{24,28},{28,32},{32,36}... | collective-permute-start | bytes 46088 | tf_op jit(solution)/shard_map/ppermute | solution.py:19
  564.5 19.9 %copy-start.19 = (f32[6,2,16]{2,1,0:T(2,128)}, f32[6,2,16]{2,1,0:T(2,128)S(1)}, u32[]{:S(2)}) copy-start(f32[6,2,16]{2,1,0:T(2,128)S(1)} %get-tuple-element.19) | copy-start | bytes 2308
  564.5 37.6 %copy-start.14 = (f32[2,16]{1,0:T(2,128)}, f32[2,16]{1,0:T(2,128)S(1)}, u32[]{:S(2)}) copy-start(f32[2,16]{1,0:T(2,128)S(1)} %get-tuple-element.21) | copy-start | bytes 388
  564.5 37.7 %copy-start.16 = (f32[2,16]{1,0:T(2,128)}, f32[2,16]{1,0:T(2,128)S(1)}, u32[]{:S(2)}) copy-start(f32[2,16]{1,0:T(2,128)S(1)} %get-tuple-element.22) | copy-start | bytes 388
  605.3 30.2 %collective-permute-start.6 = (f32[2,16,64,128]{3,2,1,0:T(8,128)S(1)}, f32[2,16,64,128]{3,2,1,0:T(8,128)}, u32[]{:S(2)}, u32[]{:S(2)}) collective-permute-start(f32[2,16,64,128]{3,2,1,0:T(8,128)S(1)} %fusion.20), channel_id=1, source_target_pairs={{0,4},{4,8},{8,12},{12,16},{16,20},{20,24},{24,28},{28,32},{32,36}... | collective-permute-start | bytes 3145736 | tf_op jit(solution)/shard_map/ppermute | solution.py:19
  635.5 29.9 %collective-permute-start.7 = (f32[2,16,64,128]{3,2,1,0:T(8,128)}, f32[2,16,64,128]{3,2,1,0:T(8,128)S(1)}, u32[]{:S(2)}, u32[]{:S(2)}) collective-permute-start(f32[2,16,64,128]{3,2,1,0:T(8,128)} %collective-permute-done.6), channel_id=1, source_target_pairs={{0,4},{4,8},{8,12},{12,16},{16,20},{20,24},{24,28},{28,32},{32,36}... | collective-permute-start | bytes 3145736 | tf_op jit(solution)/shard_map/ppermute | solution.py:19
  637.5 27.4 %collective-permute-start.1 = (f32[2,16]{1,0:T(2,128)}, f32[2,16]{1,0:T(2,128)S(1)}, u32[]{:S(2)}, u32[]{:S(2)}) collective-permute-start(f32[2,16]{1,0:T(2,128)} %get-tuple-element.25), channel_id=1, source_target_pairs={{0,4},{4,8},{8,12},{12,16},{16,20},{20,24},{24,28},{28,32},{32,36}... | collective-permute-start | bytes 392 | tf_op jit(solution)/shard_map/ppermute | solution.py:19
  666.9 25.5 %copy-start.4 = (f32[2,16,64,128]{3,2,1,0:T(8,128)}, f32[2,16,64,128]{3,2,1,0:T(8,128)S(1)}, u32[]{:S(2)}) copy-start(f32[2,16,64,128]{3,2,1,0:T(8,128)S(1)} %add_select_fusion.4) | copy-start | bytes 3145732
  666.9 27.3 %collective-permute-start.8 = (f32[2,16,64,128]{3,2,1,0:T(8,128)S(1)}, f32[2,16,64,128]{3,2,1,0:T(8,128)}, u32[]{:S(2)}, u32[]{:S(2)}) collective-permute-start(f32[2,16,64,128]{3,2,1,0:T(8,128)S(1)} %add_select_fusion.4), channel_id=1, source_target_pairs={{0,8},{4,12},{8,16},{12,20},{16,24},{20,28},{24,32},{28,36},{32,40... | collective-permute-start | bytes 3145736 | tf_op jit(solution)/shard_map/ppermute | solution.py:19
  668.8 74.8 %slice-start = ((s8[6291456]{0:T(1024)(128)(4,1)}), s8[2097152]{0:T(1024)(128)(4,1)S(1)}, s32[]{:S(2)}) async-start(s8[6291456]{0:T(1024)(128)(4,1)} %bitcast.125), calls=%async_computation.2 | async-start | bytes 4194304
  669.9 21.2 %collective-permute-start.2 = (f32[2,16]{1,0:T(2,128)}, f32[2,16]{1,0:T(2,128)S(1)}, u32[]{:S(2)}, u32[]{:S(2)}) collective-permute-start(f32[2,16]{1,0:T(2,128)} %broadcast_select_fusion), channel_id=1, source_target_pairs={{0,4},{4,8},{8,12},{12,16},{16,20},{20,24},{24,28},{28,32},{32,36}... | collective-permute-start | bytes 392 | tf_op jit(solution)/shard_map/ppermute | solution.py:19
  695.9 40.0 %collective-permute-start.9 = (f32[2,16,64,128]{3,2,1,0:T(8,128)S(1)}, f32[2,16,64,128]{3,2,1,0:T(8,128)}, u32[]{:S(2)}, u32[]{:S(2)}) collective-permute-start(f32[2,16,64,128]{3,2,1,0:T(8,128)S(1)} %add_select_fusion.3), channel_id=1, source_target_pairs={{0,16},{4,20},{8,24},{12,28},{16,32},{20,36},{24,40},{28,44},{32,4... | collective-permute-start | bytes 3145736 | tf_op jit(solution)/shard_map/ppermute | solution.py:19
  698.5 19.5 %collective-permute-start.3 = (f32[2,16]{1,0:T(2,128)}, f32[2,16]{1,0:T(2,128)}, u32[]{:S(2)}, u32[]{:S(2)}) collective-permute-start(f32[2,16]{1,0:T(2,128)} %multiply_select_fusion.3), channel_id=1, source_target_pairs={{0,8},{4,12},{8,16},{12,20},{16,24},{20,28},{24,32},{28,36},{32,40... | collective-permute-start | bytes 392 | tf_op jit(solution)/shard_map/ppermute | solution.py:19
  718.7 7.9 collective-permute-start.4
  727.1 5.6 collective-permute-start.5
  733.4 11.4 %copy-start.17 = (f32[2,16]{1,0:T(2,128)S(1)}, f32[2,16]{1,0:T(2,128)}, u32[]{:S(2)}) copy-start(f32[2,16]{1,0:T(2,128)} %copy-done.16) | copy-start | bytes 388
  737.4 22.3 %collective-permute-start.10 = (f32[2,16,64,128]{3,2,1,0:T(8,128)S(1)}, f32[2,16,64,128]{3,2,1,0:T(8,128)S(1)}, u32[]{:S(2)}, u32[]{:S(2)}) collective-permute-start(f32[2,16,64,128]{3,2,1,0:T(8,128)S(1)} %add_select_fusion.2), channel_id=1, source_target_pairs={{0,32},{4,36},{8,40},{12,44},{16,48},{20,52},{24,56},{28,60},{32,6... | collective-permute-start | bytes 3145736 | tf_op jit(solution)/shard_map/ppermute | solution.py:19
  744.8 17.3 %copy-start.5 = (bf16[6,128,2,128]{3,1,0,2:T(8,128)(2,1)S(1)}, bf16[6,128,2,128]{3,1,0,2:T(8,128)(2,1)}, u32[]{:S(2)}) copy-start(bf16[6,128,2,128]{3,1,0,2:T(8,128)(2,1)} %get-tuple-element.11) | copy-start | bytes 1179652
  744.8 17.7 %copy-start.2 = (bf16[6,128,2,1024]{1,3,2,0:T(8,128)(2,1)S(1)}, bf16[6,128,2,1024]{1,3,2,0:T(8,128)(2,1)}, u32[]{:S(2)}) copy-start(bf16[6,128,2,1024]{1,3,2,0:T(8,128)(2,1)} %copy-done.1) | copy-start | bytes 9437188
  744.8 17.7 %copy-start.8 = (f32[6,2,16,128]{3,2,1,0:T(8,128)S(1)}, f32[6,2,16,128]{3,2,1,0:T(8,128)}, u32[]{:S(2)}) copy-start(f32[6,2,16,128]{3,2,1,0:T(8,128)} %copy.53) | copy-start | bytes 294916
  744.8 17.7 %copy-start.9 = (f32[6,2,16,128]{3,2,1,0:T(8,128)S(1)}, f32[6,2,16,128]{3,2,1,0:T(8,128)}, u32[]{:S(2)}) copy-start(f32[6,2,16,128]{3,2,1,0:T(8,128)} %copy.55) | copy-start | bytes 294916
  744.8 17.7 %copy-start.11 = (pred[128,128]{1,0:T(8,128)(4,1)S(1)}, pred[128,128]{1,0:T(8,128)(4,1)}, u32[]{:S(2)}) copy-start(pred[128,128]{1,0:T(8,128)(4,1)} %iota_compare_fusion) | copy-start | bytes 49156
  760.5 22.9 %collective-permute-start.11 = (f32[2,16,64,128]{3,2,1,0:T(8,128)S(1)}, f32[2,16,64,128]{3,2,1,0:T(8,128)S(1)}, u32[]{:S(2)}, u32[]{:S(2)}) collective-permute-start(f32[2,16,64,128]{3,2,1,0:T(8,128)S(1)} %add_select_fusion.1), channel_id=1, source_target_pairs={{0,64},{4,68},{8,72},{12,76},{16,80},{20,84},{24,88},{28,92},{32,9... | collective-permute-start | bytes 3145736 | tf_op jit(solution)/shard_map/ppermute | solution.py:19
  762.1 21.5 %slice-start.2 = ((s8[6291456]{0:T(1024)(128)(4,1)}), s8[4194304]{0:T(1024)(128)(4,1)S(1)}, s32[]{:S(2)}) async-start(s8[6291456]{0:T(1024)(128)(4,1)} %bitcast.133), calls=%async_computation.4 | async-start | bytes 8388608
  762.5 21.1 %slice-start.3 = ((s8[6291456]{0:T(1024)(128)(4,1)}), s8[2097152]{0:T(1024)(128)(4,1)S(1)}, s32[]{:S(2)}) async-start(s8[6291456]{0:T(1024)(128)(4,1)} %bitcast.133), calls=%async_computation.5 | async-start | bytes 4194304
  762.5 21.1 %copy-start.7 = (f32[6,128,2,16]{1,3,2,0:T(8,128)S(1)}, f32[6,128,2,16]{1,3,2,0:T(8,128)}, u32[]{:S(2)}) copy-start(f32[6,128,2,16]{1,3,2,0:T(8,128)} %copy.56) | copy-start | bytes 294916
  762.5 21.1 %copy-start.20 = (f32[6,2,16]{2,1,0:T(2,128)S(1)}, f32[6,2,16]{2,1,0:T(2,128)}, u32[]{:S(2)}) copy-start(f32[6,2,16]{2,1,0:T(2,128)} %copy-done.19) | copy-start | bytes 2308
  762.5 21.1 %copy-start.24 = (f32[2,16]{1,0:T(2,128)S(1)}, f32[2,16]{1,0:T(2,128)}, u32[]{:S(2)}) copy-start(f32[2,16]{1,0:T(2,128)} %param.14) | copy-start | bytes 388
  (12 other events, 74.7 us)
Sparse Core Ops, SparseCore 0:
  8.9 524.0 all-gather.1
